TPU v7x, 512 devices: a whole 4x8x8 slice. The times are simulated.
512 devices in a mesh: group: 8 (over x, y_hi), sub: 64 (over y_lo, z, core).
Axes of the slice: x: 4, y: 8 (y_hi: 2, y_lo: 4; y = y_hi * 4 + y_lo), z: 8, core: 2. Of those that a mesh axis runs over, the one named last changes fastest.
Arguments:
- modes: bfloat16 [524288, 512], P(('group', 'sub')), may hold values from -6 to 6
- block_vals: bfloat16 [24576, 128, 128], P(('group', 'sub')), may hold values from -0.21875 to 0.21875
- block_cols: int32 [24576], P(('group', 'sub')), may hold values from 0 to 7, as said below
- level_maps: bfloat16 [2, 128, 128], replicated, may hold values from -0.5 to 0.5
- psi: bfloat16 [524288, 512], P(('group', 'sub')), may hold values from -0.09375 to 0.09375
- parent_vals: bfloat16 [4096, 128, 128], P(('group', 'sub')), may hold values from -0.09375 to 0.09375
- parent_rows: int32 [4096], P(('group', 'sub')), may hold values from 0 to 63
Outputs:
- parent_coupling: bfloat16 [8192, 1024], P('sub', 'group')
- projected: float32 [4096, 512], P(('group', 'sub'))
Inputs may be any that keep to these rules, and one draw needn't show every extreme that they name: `block_cols`: within one interface row block of one device the 6 vertex blocks are distinct.
All inputs are finite; a program needn't handle non-finite values.
Results may differ from a plain program's by a relative error of at most 0.0078.
Values may be sent and summed in bfloat16 or wider, within the bound.
No kernel may reach another device: no remote copies, remote signals or barrier semaphores. Data moves between devices by JAX's collectives and lax.ppermute only.
A program may use at most 64 MiB of HBM per device.

v0:
```python
import jax
import jax.numpy as jnp
from jax import lax
from jax.sharding import PartitionSpec as P

IFB = 8
BPR = 6


def from_partner(value, axis, distance):
    mask = 2**distance
    pairs = [(source, source ^ mask) for source in range(lax.axis_size(axis))]
    return lax.ppermute(value, axis, pairs)


def on_device(modes, block_vals, block_cols, level_maps, psi, parent_vals, parent_rows):
    block_size = block_vals.shape[1]
    width = modes.shape[1]
    vertex_blocks = modes.shape[0] // block_size
    row_blocks = IFB
    levels = min(2, lax.axis_size("group").bit_length() - 1)
    group_index = lax.axis_index("group")
    onehot = (
        block_cols.reshape(row_blocks, BPR)[:, :, None] == jnp.arange(vertex_blocks)[None, None, :]
    ).astype(jnp.float32)
    blocks = block_vals.astype(jnp.float32).reshape(row_blocks, BPR, block_size, block_size)
    dense = (
        jnp.einsum("rbc,rbij->ricj", onehot, blocks)
        .reshape(row_blocks * block_size, vertex_blocks * block_size)
        .astype(jnp.bfloat16)
    )
    panel = jnp.dot(dense, modes, preferred_element_type=jnp.float32).astype(jnp.bfloat16)
    for level in range(levels):
        sibling = from_partner(panel, "group", level)
        total = (panel.astype(jnp.float32) + sibling.astype(jnp.float32)).astype(jnp.bfloat16)
        mapped = jnp.einsum(
            "ab,rbm->ram",
            level_maps[level],
            total.reshape(row_blocks, block_size, width),
            preferred_element_type=jnp.float32,
        )
        panel = mapped.reshape(row_blocks * block_size, width).astype(jnp.bfloat16)
    head = panel[:block_size]
    piece = lax.all_gather(head, "sub", axis=0, tiled=True)
    owners_here = piece.shape[0] // block_size
    owners = jnp.arange(owners_here)
    select = (parent_rows[:, None] == owners[None, :]).astype(jnp.bfloat16)
    picked = jnp.einsum(
        "kj,jbm->kbm",
        select,
        piece.reshape(owners_here, block_size, width),
        preferred_element_type=jnp.float32,
    ).astype(jnp.bfloat16)
    partial_sum = jnp.einsum("kab,kbm->am", parent_vals, picked, preferred_element_type=jnp.float32)
    for level in reversed(range(levels)):
        half = partial_sum.shape[1] // 2
        upper = group_index >> level & 1
        keeper = lax.dynamic_slice_in_dim(partial_sum, upper * half, half, 1)
        sender = lax.dynamic_slice_in_dim(partial_sum, (1 - upper) * half, half, 1)
        partial_sum = keeper + from_partner(sender, "group", level)
    parent_out = partial_sum.astype(jnp.bfloat16)
    projected = lax.psum_scatter(
        lax.dot_general(psi, panel, (((0,), (0,)), ((), ())), preferred_element_type=jnp.float32),
        "sub",
        scatter_dimension=0,
        tiled=True,
    )
    return (parent_out, projected)


def solution(mesh):
    return jax.shard_map(
        on_device,
        mesh=mesh,
        in_specs=(
            P(("group", "sub"), None),
            P(("group", "sub"), None, None),
            P(("group", "sub")),
            P(),
            P(("group", "sub"), None),
            P(("group", "sub"), None, None),
            P(("group", "sub")),
        ),
        out_specs=(P("sub", "group"), P(("group", "sub"), None)),
        check_vma=False,
    )
```

profile of v0, /device:TPU:2, one launch (start us, length us, event | category | flops | bytes accessed | tf_op | source)
XLA Modules:
  0.0 514.9 jit_solution(13691395936488366939)
XLA Ops:
  7.2 0.8 eq.31
  8.1 0.5 copy-done
  8.6 1.0 fusion.7
  9.8 1.2 fusion.10
  11.1 7.9 %collective-permute-start = (bf16[1024,512]{1,0:T(8,128)(2,1)S(1)}, bf16[1024,512]{1,0:T(8,128)(2,1)S(1)}, u32[]{:S(2)}, u32[]{:S(2)}) collective-permute-start(bf16[1024,512]{1,0:T(8,128)(2,1)S(1)} %fusion.10), channel_id=1, source_target_pairs={{0,64},{64,0},{128,192},{192,128},{256,320},{320,256},{384,448},{4... | collective-permute-start | bytes 3145736 | tf_op jit(solution)/shard_map/ppermute | solution.py:13
  19.0 45.1 %collective-permute-done = bf16[1024,512]{1,0:T(8,128)(2,1)S(1)} collective-permute-done((bf16[1024,512]{1,0:T(8,128)(2,1)S(1)}, bf16[1024,512]{1,0:T(8,128)(2,1)S(1)}, u32[]{:S(2)}, u32[]{:S(2)}) %collective-permute-start) | collective-permute-done | bytes 1048608 | tf_op jit(solution)/shard_map/ppermute | solution.py:13
  64.4 0.4 convolution_convert_fusion.1
  64.8 2.4 collective-permute-start.1
  67.2 14.2 %collective-permute-done.1 = bf16[1024,512]{1,0:T(8,128)(2,1)S(1)} collective-permute-done((bf16[1024,512]{1,0:T(8,128)(2,1)S(1)}, bf16[1024,512]{1,0:T(8,128)(2,1)S(1)}, u32[]{:S(2)}, u32[]{:S(2)}) %collective-permute-start.1) | collective-permute-done | bytes 1048608 | tf_op jit(solution)/shard_map/ppermute | solution.py:13
  81.5 0.4 add_convert_fusion
  81.9 0.4 convolution_convert_fusion
  82.3 0.7 slice.16
  83.2 2.9 convolution_bitcast_fusion
  86.1 2.6 copy.18
  88.8 130.8 %all-gather.3.cloned.1.call-done = bf16[1,8192,512]{2,1,0:T(8,128)(2,1)} async-done(((bf16[1,128,512]{2,1,0:T(8,128)(2,1)}), bf16[1,8192,512]{2,1,0:T(8,128)(2,1)}) %all-gather.3.cloned.1.call-update) | async-done | bytes 8388624 | tf_op jit(solution)/shard_map/all_gather | solution.py:44
  219.6 12.2 %fusion = bf16[8,128,512]{2,0,1:T(8,128)(2,1)S(1)} fusion(bf16[64,128,512]{2,1,0:T(8,128)(2,1)} %bitcast.52, s32[8]{0:T(128)S(1)} %copy-done.3), kind=kOutput, calls=%fused_computation | convolution fusion | flops 67109376 | bytes 9437216 | tf_op jit(solution)/shard_map/kj,jbm->kbm/dot_general | solution.py:48
  231.8 1.7 copy.17
  233.5 1.7 convolution_bitcast_fusion.1
  235.2 2.5 collective-permute-start.2
  237.7 5.0 collective-permute-done.2
  242.8 8.1 %collective-permute-start.3 = (f32[128,128]{0,1:T(8,128)S(1)}, f32[128,128]{0,1:T(8,128)S(1)}, u32[]{:S(2)}, u32[]{:S(2)}) collective-permute-start(f32[128,128]{0,1:T(8,128)S(1)} %constant_dynamic-slice_fusion), channel_id=1, source_target_pairs={{0,64},{64,0},{128,192},{192,128},{256,320},{320,256},{384,448},{4... | collective-permute-start | bytes 196616 | tf_op jit(solution)/shard_map/ppermute | solution.py:13
  250.8 2.2 collective-permute-done.3
  253.1 0.7 copy.13
  253.8 254.3 %reduce-scatter.4.cloned.1.call-done = f32[8,512]{1,0:T(8,128)} async-done(((f32[512,512]{1,0:T(8,128)}), f32[8,512]{1,0:T(8,128)}) %reduce-scatter.4.cloned.1.call-update) | async-done | bytes 16400
  (18 shorter events, 0.9 us)
Async XLA Ops:
  7.2 1.4 copy-start
  7.2 212.4 %all-gather.3.cloned.1.call-start = ((), (), s32[]{:S(2)}) async-start(), calls=%async_computation.1 | async-start | bytes 8519680 | tf_op jit(solution)/shard_map/all_gather | solution.py:44
  8.6 1.2 copy-start.4
  11.1 53.3 %copy-start.2 = (bf16[2,128,128]{2,1,0:T(8,128)(2,1)S(1)}, bf16[2,128,128]{2,1,0:T(8,128)(2,1)}, u32[]{:S(2)}) copy-start(bf16[2,128,128]{2,1,0:T(8,128)(2,1)} %param.10) | copy-start | bytes 196612
  11.1 53.0 %collective-permute-start = (bf16[1024,512]{1,0:T(8,128)(2,1)S(1)}, bf16[1024,512]{1,0:T(8,128)(2,1)S(1)}, u32[]{:S(2)}, u32[]{:S(2)}) collective-permute-start(bf16[1024,512]{1,0:T(8,128)(2,1)S(1)} %fusion.10), channel_id=1, source_target_pairs={{0,64},{64,0},{128,192},{192,128},{256,320},{320,256},{384,448},{4... | collective-permute-start | bytes 3145736 | tf_op jit(solution)/shard_map/ppermute | solution.py:13
  64.8 16.7 %collective-permute-start.1 = (bf16[1024,512]{1,0:T(8,128)(2,1)S(1)}, bf16[1024,512]{1,0:T(8,128)(2,1)S(1)}, u32[]{:S(2)}, u32[]{:S(2)}) collective-permute-start(bf16[1024,512]{1,0:T(8,128)(2,1)S(1)} %bitcast.53), channel_id=1, source_target_pairs={{0,128},{64,192},{128,0},{192,64},{256,384},{320,448},{384,256},{4... | collective-permute-start | bytes 3145736 | tf_op jit(solution)/shard_map/ppermute | solution.py:13
  83.0 425.1 %reduce-scatter.4.cloned.1.call-start = ((), (), s32[]{:S(2)}) async-start(), calls=%async_computation.2 | async-start | bytes 1064960
  86.1 133.4 %copy-start.3 = (s32[8]{0:T(128)S(1)}, s32[8]{0:T(128)}, u32[]{:S(2)}) copy-start(s32[8]{0:T(128)} %param.13) | copy-start | bytes 100
  231.8 1.7 copy-start.1
  235.2 7.5 %collective-permute-start.2 = (f32[128,256]{0,1:T(8,128)S(1)}, f32[128,256]{0,1:T(8,128)S(1)}, u32[]{:S(2)}, u32[]{:S(2)}) collective-permute-start(f32[128,256]{0,1:T(8,128)S(1)} %dynamic-slice_bitcast_fusion), channel_id=1, source_target_pairs={{0,128},{64,192},{128,0},{192,64},{256,384},{320,448},{384,256},{4... | collective-permute-start | bytes 393224 | tf_op jit(solution)/shard_map/ppermute | solution.py:13
  242.8 10.3 %collective-permute-start.3 = (f32[128,128]{0,1:T(8,128)S(1)}, f32[128,128]{0,1:T(8,128)S(1)}, u32[]{:S(2)}, u32[]{:S(2)}) collective-permute-start(f32[128,128]{0,1:T(8,128)S(1)} %constant_dynamic-slice_fusion), channel_id=1, source_target_pairs={{0,64},{64,0},{128,192},{192,128},{256,320},{320,256},{384,448},{4... | collective-permute-start | bytes 196616 | tf_op jit(solution)/shard_map/ppermute | solution.py:13
Sparse Core Ops, SparseCore 0:
  83.1 136.4 all-gather.2
  222.9 285.1 reduce-scatter.3
where the time goes:
time: 515 us
  waiting for transfers between devices  452 us (88%)
  starting transfers between devices  21.1 us (4%)
  matrix products  19.9 us (4%)
  between operations  14.2 us (3%)
  local copies, waits for them, and re-layouts  7.35 us (1%)
    unnamed x3, waiting for transfers between devices  254 us
    all_gather x1, waiting for transfers between devices, on_device(): piece = lax.all_gather(head, 'sub', axis=0, tiled=True)  131 us
    ppermute x4, waiting for transfers between devices, from_partner(): return lax.ppermute(value, axis, pairs)  66.6 us
    ppermute x4, starting transfers between devices, from_partner(): return lax.ppermute(value, axis, pairs)  20.8 us
    dot_general x1, matrix products, on_device(): jnp.einsum('kj,jbm->kbm', select, piece.reshape(owners_here, block_size,...  12.2 us
  transfers between devices with their start and end apart: 6, of which 6 were waited for; matrix products, arithmetic and copies ran while one was open for 4% of the time, Pallas kernels for 0%

commit v1 on v0

--- a/solution.py
+++ b/solution.py
@@ -5,6 +5,15 @@
 
 IFB = 8
 BPR = 6
+
+
+def _form_frame(u):
+    return jnp.concatenate(
+        jax.lax.all_to_all(
+            jnp.stack([u for _ in range(jax.lax.axis_size("sub"))], axis=0), "sub", 0, 0
+        ),
+        axis=0,
+    )
 
 
 def from_partner(value, axis, distance):
@@ -41,7 +50,7 @@
         )
         panel = mapped.reshape(row_blocks * block_size, width).astype(jnp.bfloat16)
     head = panel[:block_size]
-    piece = lax.all_gather(head, "sub", axis=0, tiled=True)
+    piece = _form_frame(head)
     owners_here = piece.shape[0] // block_size
     owners = jnp.arange(owners_here)
     select = (parent_rows[:, None] == owners[None, :]).astype(jnp.bfloat16)

time: 515 us -> 556 us (1.080)
  the two profiles are of different devices: /device:TPU:2 before, /device:TPU:4 now
where the time goes in v1:
time: 556 us; the launch traced here: 555 us
  waiting for transfers between devices  454 us (82%)
  starting transfers between devices  55.9 us (10%)
  matrix products  20 us (4%)
  between operations  14.2 us (3%)
  local copies, waits for them, and re-layouts  10.9 us (2%)
    all_to_all x1, waiting for transfers between devices, _form_frame(): jax.lax.all_to_all(jnp.stack([u for _ in range(jax.lax.axis_size('sub'))]...  215 us
    unnamed x2, waiting for transfers between devices  173 us
    ppermute x4, waiting for transfers between devices, from_partner(): return lax.ppermute(value, axis, pairs)  65.8 us
    ppermute x4, starting transfers between devices, from_partner(): return lax.ppermute(value, axis, pairs)  31.5 us
    all_to_all x1, starting transfers between devices, _form_frame(): jax.lax.all_to_all(jnp.stack([u for _ in range(jax.lax.axis_size('sub'))]...  24.2 us
    dot_general x1, matrix products, on_device(): jnp.einsum('kj,jbm->kbm', select, piece.reshape(owners_here, block_size,...  12.2 us
  transfers between devices with their start and end apart: 6, of which 6 were waited for; matrix products, arithmetic and copies ran while one was open for 4% of the time, Pallas kernels for 0%

profile of v1, /device:TPU:4, one launch (start us, length us, event | category | flops | bytes accessed | tf_op | source)
XLA Modules:
  0.0 555.2 jit_solution(11249220287774609341)
XLA Ops:
  7.2 0.8 eq.31
  8.0 0.6 copy-done
  8.6 1.0 fusion.7
  9.8 1.2 fusion.10
  11.1 7.9 %collective-permute-start = (bf16[1024,512]{1,0:T(8,128)(2,1)S(1)}, bf16[1024,512]{1,0:T(8,128)(2,1)S(1)}, u32[]{:S(2)}, u32[]{:S(2)}) collective-permute-start(bf16[1024,512]{1,0:T(8,128)(2,1)S(1)} %fusion.10), channel_id=1, source_target_pairs={{0,64},{64,0},{128,192},{192,128},{256,320},{320,256},{384,448},{4... | collective-permute-start | bytes 3145736 | tf_op jit(solution)/shard_map/ppermute | solution.py:22
  18.9 45.1 %collective-permute-done = bf16[1024,512]{1,0:T(8,128)(2,1)S(1)} collective-permute-done((bf16[1024,512]{1,0:T(8,128)(2,1)S(1)}, bf16[1024,512]{1,0:T(8,128)(2,1)S(1)}, u32[]{:S(2)}, u32[]{:S(2)}) %collective-permute-start) | collective-permute-done | bytes 1048608 | tf_op jit(solution)/shard_map/ppermute | solution.py:22
  64.4 0.4 convolution_convert_fusion.1
  64.8 3.1 collective-permute-start.1
  67.9 13.6 %collective-permute-done.1 = bf16[1024,512]{1,0:T(8,128)(2,1)S(1)} collective-permute-done((bf16[1024,512]{1,0:T(8,128)(2,1)S(1)}, bf16[1024,512]{1,0:T(8,128)(2,1)S(1)}, u32[]{:S(2)}, u32[]{:S(2)}) %collective-permute-start.1) | collective-permute-done | bytes 1048608 | tf_op jit(solution)/shard_map/ppermute | solution.py:22
  81.9 0.4 convolution_convert_fusion
  82.3 4.3 stack.2
  86.6 24.2 %all-to-all-start = ((bf16[64,128,512]{2,1,0:T(8,128)(2,1)}), bf16[64,128,512]{2,1,0:T(8,128)(2,1)}, u32[]{:S(2)}, u32[]{:S(2)}) async-start(bf16[64,128,512]{2,1,0:T(8,128)(2,1)} %stack.2), calls=%async_computation | async-start | bytes 16777216 | tf_op jit(solution)/shard_map/all_to_all | solution.py:12
  111.0 3.0 convolution_bitcast_fusion
  114.0 2.6 copy.18
  116.6 215.0 %all-to-all-done = bf16[64,128,512]{2,1,0:T(8,128)(2,1)} async-done(((bf16[64,128,512]{2,1,0:T(8,128)(2,1)}), bf16[64,128,512]{2,1,0:T(8,128)(2,1)}, u32[]{:S(2)}, u32[]{:S(2)}) %all-to-all-start) | async-done | bytes 8388640 | tf_op jit(solution)/shard_map/all_to_all | solution.py:12
  331.6 12.2 %fusion = bf16[8,128,512]{2,0,1:T(8,128)(2,1)S(1)} fusion(bf16[64,128,512]{2,1,0:T(8,128)(2,1)} %all-to-all-done, s32[8]{0:T(128)S(1)} %copy-done.3), kind=kOutput, calls=%fused_computation | convolution fusion | flops 67109376 | bytes 9437216 | tf_op jit(solution)/shard_map/kj,jbm->kbm/dot_general | solution.py:57
  343.9 1.7 copy.17
  345.6 1.7 convolution_bitcast_fusion.1
  347.2 1.9 collective-permute-start.2
  349.2 4.9 collective-permute-done.2
  354.1 18.6 %collective-permute-start.3 = (f32[128,128]{0,1:T(8,128)S(1)}, f32[128,128]{0,1:T(8,128)S(1)}, u32[]{:S(2)}, u32[]{:S(2)}) collective-permute-start(f32[128,128]{0,1:T(8,128)S(1)} %constant_dynamic-slice_fusion), channel_id=1, source_target_pairs={{0,64},{64,0},{128,192},{192,128},{256,320},{320,256},{384,448},{4... | collective-permute-start | bytes 196616 | tf_op jit(solution)/shard_map/ppermute | solution.py:22
  372.7 2.2 collective-permute-done.3
  375.0 0.7 copy.13
  375.7 172.6 %reduce-scatter.4.cloned.1.call-done = f32[8,512]{1,0:T(8,128)} async-done(((f32[512,512]{1,0:T(8,128)}), f32[8,512]{1,0:T(8,128)}) %reduce-scatter.4.cloned.1.call-update) | async-done | bytes 16400
  (18 shorter events, 1.2 us)
Async XLA Ops:
  7.2 1.4 copy-start
  8.6 1.2 copy-start.4
  11.1 53.3 %copy-start.2 = (bf16[2,128,128]{2,1,0:T(8,128)(2,1)S(1)}, bf16[2,128,128]{2,1,0:T(8,128)(2,1)}, u32[]{:S(2)}) copy-start(bf16[2,128,128]{2,1,0:T(8,128)(2,1)} %param.10) | copy-start | bytes 196612
  11.1 53.0 %collective-permute-start = (bf16[1024,512]{1,0:T(8,128)(2,1)S(1)}, bf16[1024,512]{1,0:T(8,128)(2,1)S(1)}, u32[]{:S(2)}, u32[]{:S(2)}) collective-permute-start(bf16[1024,512]{1,0:T(8,128)(2,1)S(1)} %fusion.10), channel_id=1, source_target_pairs={{0,64},{64,0},{128,192},{192,128},{256,320},{320,256},{384,448},{4... | collective-permute-start | bytes 3145736 | tf_op jit(solution)/shard_map/ppermute | solution.py:22
  64.8 16.7 %collective-permute-start.1 = (bf16[1024,512]{1,0:T(8,128)(2,1)S(1)}, bf16[1024,512]{1,0:T(8,128)(2,1)S(1)}, u32[]{:S(2)}, u32[]{:S(2)}) collective-permute-start(bf16[1024,512]{1,0:T(8,128)(2,1)S(1)} %bitcast.53), channel_id=1, source_target_pairs={{0,128},{64,192},{128,0},{192,64},{256,384},{320,448},{384,256},{4... | collective-permute-start | bytes 3145736 | tf_op jit(solution)/shard_map/ppermute | solution.py:22
  86.6 245.0 %all-to-all-start = ((bf16[64,128,512]{2,1,0:T(8,128)(2,1)}), bf16[64,128,512]{2,1,0:T(8,128)(2,1)}, u32[]{:S(2)}, u32[]{:S(2)}) async-start(bf16[64,128,512]{2,1,0:T(8,128)(2,1)} %stack.2), calls=%async_computation | async-start | bytes 16777216 | tf_op jit(solution)/shard_map/all_to_all | solution.py:12
  110.8 437.6 %reduce-scatter.4.cloned.1.call-start = ((), (), s32[]{:S(2)}) async-start(), calls=%async_computation.2 | async-start | bytes 1064960
  114.0 217.6 %copy-start.3 = (s32[8]{0:T(128)S(1)}, s32[8]{0:T(128)}, u32[]{:S(2)}) copy-start(s32[8]{0:T(128)} %param.13) | copy-start | bytes 100
  343.9 1.7 copy-start.1
  347.2 6.9 %collective-permute-start.2 = (f32[128,256]{0,1:T(8,128)S(1)}, f32[128,256]{0,1:T(8,128)S(1)}, u32[]{:S(2)}, u32[]{:S(2)}) collective-permute-start(f32[128,256]{0,1:T(8,128)S(1)} %dynamic-slice_bitcast_fusion), channel_id=1, source_target_pairs={{0,128},{64,192},{128,0},{192,64},{256,384},{320,448},{384,256},{4... | collective-permute-start | bytes 393224 | tf_op jit(solution)/shard_map/ppermute | solution.py:22
  354.1 20.8 %collective-permute-start.3 = (f32[128,128]{0,1:T(8,128)S(1)}, f32[128,128]{0,1:T(8,128)S(1)}, u32[]{:S(2)}, u32[]{:S(2)}) collective-permute-start(f32[128,128]{0,1:T(8,128)S(1)} %constant_dynamic-slice_fusion), channel_id=1, source_target_pairs={{0,64},{64,0},{128,192},{192,128},{256,320},{320,256},{384,448},{4... | collective-permute-start | bytes 196616 | tf_op jit(solution)/shard_map/ppermute | solution.py:22
Sparse Core Ops, SparseCore 0:
  116.7 431.6 reduce-scatter.3
